TPU v7x, 32 devices: a whole 2x2x4 slice. The times are simulated.
32 devices in a mesh: groups: 2 (over y), gx: 4 (over z), gz: 2 (over x), vert: 2 (over core).
Axes of the slice: x: 2, y: 2, z: 4, core: 2. Of those that a mesh axis runs over, the one named last changes fastest.
Arguments:
- flow_field: bfloat16 [4, 4, 5, 4, 256, 256], P('groups', 'vert', None, 'gx', None, 'gz'), parts along dimension 0, may hold values from -6 to 6
- test_streams: int32 [4], P('groups'), parts along dimension 0, may hold values from 0 to 999999
- snapshot_ids: int32 [4, 4], P('groups', 'vert'), parts along dimension 0, may hold values from 0 to 65535
Outputs:
- sketch_x: float32 [8, 128], P(('groups', 'gx')), parts along dimension 0
- sketch_y: float32 [512, 128], P(('groups', 'gx', 'gz', 'vert')), parts along dimension 0
- sketch_z: float32 [512, 128], P(('groups', 'gz'), ('gx', 'vert')), parts along dimension 0
- core_sketch: float32 [4608, 2, 48], P(('groups', 'gx')), parts along dimension 0
There are 2 independent parts, one for each index of `groups`. A program takes and returns all parts, laid end to end along the dimension named above; each array names one. Nothing has to cross between parts.
All inputs are finite; a program needn't handle non-finite values.
Results may differ from a plain program's by a relative error of at most 0.007.
Values sent between devices are 32-bit elements; how exact they have to be, the bound alone decides.
No kernel may reach another device: no remote copies, remote signals or barrier semaphores. Data moves between devices by JAX's collectives and lax.ppermute only.
A program may use at most 64 MiB of HBM per device.

v0:
```python
import math
import jax
import jax.numpy as jnp
from jax import lax
from jax.sharding import PartitionSpec as P

K = 128
S = 48
E = 2


def hash_index(index, stream, salt):
    mixed = index * -1640531535 + stream * -2048144777 + salt
    mixed = jnp.bitwise_xor(mixed, lax.shift_right_logical(mixed, jnp.int32(16)))
    mixed = mixed * 739982445
    mixed = jnp.bitwise_xor(mixed, lax.shift_right_logical(mixed, jnp.int32(13)))
    mixed = mixed * 695872825
    return jnp.bitwise_xor(mixed, lax.shift_right_logical(mixed, jnp.int32(16)))


def unit_value(index, stream, salt):
    upper = lax.shift_right_logical(hash_index(index, stream, salt), jnp.int32(9))
    return ((2 * upper + 1).astype(jnp.float32) * 2.0 ** (-24) - 1.0).astype(jnp.bfloat16)


def test_table(row_ids, col_ids, stride, stream, salt):
    return unit_value(row_ids[:, None] * stride + col_ids[None, :], stream, salt)


def shards(flow_field, test_streams, snapshot_ids):
    highest = lax.Precision.HIGHEST
    batches, local_snaps, variables, cells_x, cells_y, cells_z = flow_field.shape
    slabs_x = lax.axis_size("gx")
    total_x = cells_x * slabs_x
    total_z = cells_z * lax.axis_size("gz")
    total_q = variables * batches * local_snaps * lax.axis_size("vert")
    factor_stream = test_streams[0]
    core_stream = test_streams[1]
    rank_ids = jnp.arange(K, dtype=jnp.int32)
    sketch_ids = jnp.arange(S, dtype=jnp.int32)
    x_ids = lax.axis_index("gx") * cells_x + jnp.arange(cells_x, dtype=jnp.int32)
    y_ids = jnp.arange(cells_y, dtype=jnp.int32)
    z_ids = lax.axis_index("gz") * cells_z + jnp.arange(cells_z, dtype=jnp.int32)
    ax_tab = test_table(x_ids, rank_ids, K, factor_stream, 1).astype(jnp.float32)
    ay_low = test_table(y_ids, rank_ids, K, factor_stream, 2)
    az_low = test_table(z_ids, rank_ids, K, factor_stream, 3)
    ay_tab = ay_low.astype(jnp.float32)
    phy_low = test_table(sketch_ids, y_ids, cells_y, core_stream, 6)
    phz_low = test_table(sketch_ids, z_ids, total_z, core_stream, 7)

    def batch_terms(batch_idx):
        blocks = flow_field[batch_idx].reshape(-1, cells_x, cells_y, cells_z)
        pairs = blocks.shape[0]
        q_ids = (
            snapshot_ids[batch_idx][:, None] * variables
            + jnp.arange(variables, dtype=jnp.int32)[None, :]
        ).reshape(-1)
        aq_tab = test_table(q_ids, rank_ids, K, factor_stream, 4).astype(jnp.float32)
        phq_low = test_table(q_ids, jnp.arange(E, dtype=jnp.int32), E, core_stream, 8)
        rows_z = blocks.reshape(-1, cells_z)
        along_z = jnp.dot(rows_z, az_low, preferred_element_type=jnp.float32).reshape(
            pairs, cells_x, cells_y, K
        )
        along_y = jnp.einsum("qxyz,yk->qxzk", blocks, ay_low, preferred_element_type=jnp.float32)
        weights = aq_tab[:, None, :] * ax_tab[None, :, :]
        part_x = jnp.sum(
            jnp.sum(along_z * ay_tab[None, None, :, :], axis=2) * aq_tab[:, None, :], axis=0
        )
        part_y = jnp.sum(along_z * weights[:, :, None, :], axis=(0, 1))
        part_z = jnp.sum(along_y * weights[:, :, None, :], axis=(0, 1))
        first = jnp.dot(rows_z, phz_low.T, preferred_element_type=jnp.float32).reshape(
            pairs, cells_x, cells_y, S
        )
        second = jnp.einsum("qxyc,by->qxbc", first, phy_low.astype(jnp.float32), precision=highest)
        partial_core = jnp.einsum(
            "qxbc,qe->bcex", second, phq_low.astype(jnp.float32), precision=highest
        )
        return (part_x, part_y, part_z, partial_core.reshape(S * S, E, cells_x))

    def finish(part_x, part_y, part_z, partial_core):
        summed, sum_x = lax.psum((partial_core, part_x), ("gz", "vert"))
        phx_whole = test_table(
            sketch_ids, jnp.arange(total_x, dtype=jnp.int32), total_x, core_stream, 5
        ).astype(jnp.float32)
        core = jnp.einsum(
            "rex,ax->rea",
            lax.all_to_all(summed, "gx", split_axis=0, concat_axis=2, tiled=True),
            phx_whole,
            precision=highest,
        )
        sum_z = lax.psum_scatter(part_z, ("gx", "vert"), scatter_dimension=1, tiled=True)
        sum_y = lax.psum_scatter(part_y, ("gx", "gz", "vert"), scatter_dimension=0, tiled=True)
        return (sum_x, sum_y, sum_z, core)

    terms = [batch_terms(batch_idx) for batch_idx in range(batches)]
    totals = finish(terms[0][0], terms[0][1], terms[0][2], terms[0][3])
    for later in terms[1:]:
        latest = finish(later[0], later[1], later[2], later[3])
        totals = tuple((earlier + newer for earlier, newer in zip(totals, latest)))
    scale_x = 3.0**1.5 / math.sqrt(cells_y * total_z * total_q)
    scale_y = 3.0**1.5 / math.sqrt(total_x * total_z * total_q)
    scale_z = 3.0**1.5 / math.sqrt(total_x * cells_y * total_q)
    scale_core = 9.0 / math.sqrt(total_x * cells_y * total_z * total_q)
    return (totals[0] * scale_x, totals[1] * scale_y, totals[2] * scale_z, totals[3] * scale_core)


def solution(mesh):
    in_specs = (P("groups", "vert", None, "gx", None, "gz"), P("groups"), P("groups", "vert"))
    out_specs = (
        P(("groups", "gx"), None),
        P(("groups", "gx", "gz", "vert"), None),
        P(("groups", "gz"), ("gx", "vert")),
        P(("groups", "gx"), None, None),
    )
    return jax.shard_map(shards, mesh=mesh, in_specs=in_specs, out_specs=out_specs, check_vma=False)
```

profile of v0, /device:TPU:0, one launch (start us, length us, event | category | flops | bytes accessed | tf_op | source)
XLA Modules:
  0.0 124.9 jit_solution(1838660358389235373)
XLA Ops:
  7.2 1.3 %fusion.295 = (s32[1]{0:T(128)}, s32[1]{0:T(128)}) fusion(s32[2]{0:T(128)} %param.4), kind=kLoop, calls=%fused_computation.343 | loop fusion | bytes 16 | tf_op jit(solution)/shard_map/slice | solution.py:38
  8.5 0.8 multiply_bitcast_fusion
  9.6 1.4 %fusion.294 = (bf16[1,2,5,1,256,128]{5,4,3,2,1,0:T(8,128)(2,1)S(1)}, bf16[1,2,5,1,256,128]{5,4,3,2,1,0:T(8,128)(2,1)S(1)}) fusion(bf16[2,2,5,1,256,128]{5,4,3,2,1,0:T(8,128)(2,1)} %param.3), kind=kLoop, calls=%fused_computation.342 | loop fusion | bytes 2621440 | tf_op jit(solution)/shard_map/slice | solution.py:52
  13.8 1.2 fusion.68
  15.8 1.5 %convolution_bitcast_fusion.1 = f32[2560,128]{0,1:T(8,128)} fusion(bf16[2560,128]{1,0:T(8,128)(2,1)S(1)} %bitcast.111, s32[]{:T(128)} %bitcast, s32[128]{0:T(128)S(1)} %broadcast_multiply_fusion.3), kind=kOutput, calls=%fused_computation.1 | convolution fusion | flops 84197376 | bytes 1966596 | tf_op jit(solution)/shard_map/dot_general | solution.py:61
  19.8 1.5 %copy.24 = f32[2560,128]{1,0:T(8,128)} copy(f32[2560,128]{0,1:T(8,128)S(1)} %convolution_bitcast_fusion) | data formatting | bytes 2621440 | tf_op jit(solution)/shard_map/dot_general | solution.py:61
  21.2 1.5 %copy.22 = f32[2560,128]{1,0:T(8,128)} copy(f32[2560,128]{0,1:T(8,128)S(1)} %copy-done) | data formatting | bytes 2621440 | tf_op jit(solution)/shard_map/dot_general | solution.py:61
  22.7 1.7 %multiply_reduce_fusion = (f32[256,128]{1,0:T(8,128)S(1)}, f32[10,128]{1,0:T(8,128)S(1)}, f32[10,128]{1,0:T(8,128)S(1)}, f32[256,128]{1,0:T(8,128)S(1)}) fusion(f32[10,1,256,128]{3,2,0,1:T(8,128)S(1)} %bitcast.115, f32[10,128]{1,0:T(8,128)S(1)} %get-tuple-element.23, f32[256,128]{1,0:T(8,128)S(1)} %copy.23, f32[10,1,256,128]{3,2,0,1:T(8,128)} %bitcast.116, ...), kind=kLoop, calls=%fused_computation.2 | loop fusion | flops 2553344 | bytes 3035136 | tf_op jit(solution)/shard_map/reduce_sum | solution.py:69
  24.6 13.2 %all-reduce = (f32[1,128]{1,0:T(1,128)S(1)}, f32[2304,2,1]{0,1,2:T(2,128)S(1)}, f32[2304,2,1]{0,1,2:T(2,128)S(1)}) all-reduce(f32[1,128]{1,0:T(1,128)S(1)} %add_bitcast_fusion, f32[2304,2,1]{0,1,2:T(2,128)S(1)} %reshape.486, f32[2304,2,1]{0,1,2:T(2,128)S(1)} %reshape.489), channel_id=1, replica_groups=mesh['groups'=2,'gx'=4,'gz'=2,'vert'=2] {'gz','vert'}, use_global_device_ids=true, to_apply=%region_2.0 | all-reduce | flops 9344 | bytes 74752 | tf_op jit(solution)/shard_map/psum | solution.py:81
  37.7 1.5 %copy.28 = f32[2304,2,1]{1,2,0:T(1,128)S(1)} copy(f32[2304,2,1]{0,1,2:T(2,128)S(1)} %get-tuple-element.9) | data formatting | bytes 36864 | tf_op jit(solution)/shard_map/psum | solution.py:81
  39.8 10.4 %reduce.10 = f32[2304,2]{1,0:T(8,128)S(1)} reduce(f32[2304,1,2]{2,1,0:T(1,128)S(1)} %bitcast.117, f32[]{:T(128)} %broadcast.1041), dimensions={1}, to_apply=%bitcast.99.reduce_sub_computation | reduce | bytes 36868
  50.2 1.3 %reshape.496 = f32[4,1,1152]{2,1,0:T(1,128)} reshape(f32[2304,2]{1,0:T(8,128)S(1)} %reduce.10) | data formatting | bytes 36864
  51.5 4.9 %all-to-all-start = ((f32[4,1,1152]{2,1,0:T(1,128)}), f32[4,1,1152]{2,1,0:T(1,128)S(1)}, u32[]{:S(2)}, u32[]{:S(2)}) async-start(f32[4,1,1152]{2,1,0:T(1,128)} %reshape.496), calls=%async_computation | async-start | bytes 36864 | tf_op jit(solution)/shard_map/all_to_all | solution.py:87
  57.6 1.4 %copy.33 = f32[2304,2,1]{1,2,0:T(1,128)S(1)} copy(f32[2304,2,1]{0,1,2:T(2,128)S(1)} %get-tuple-element.10) | data formatting | bytes 36864 | tf_op jit(solution)/shard_map/psum | solution.py:81
  59.1 10.4 %reduce.12 = f32[2304,2]{1,0:T(8,128)S(1)} reduce(f32[2304,1,2]{2,1,0:T(1,128)S(1)} %bitcast.118, f32[]{:T(128)} %broadcast.1041), dimensions={1}, to_apply=%bitcast.101.reduce_sub_computation | reduce | bytes 36868
  69.5 1.3 %reshape.498 = f32[4,1,1152]{2,1,0:T(1,128)} reshape(f32[2304,2]{1,0:T(8,128)S(1)} %reduce.12) | data formatting | bytes 36864
  70.8 5.1 %all-to-all-start.1 = ((f32[4,1,1152]{2,1,0:T(1,128)}), f32[4,1,1152]{2,1,0:T(1,128)S(1)}, u32[]{:S(2)}, u32[]{:S(2)}) async-start(f32[4,1,1152]{2,1,0:T(1,128)} %reshape.498), calls=%async_computation.1 | async-start | bytes 36864 | tf_op jit(solution)/shard_map/all_to_all | solution.py:87
  76.6 1.8 %reshape.497 = f32[2304,1,2]{2,1,0:T(1,128)S(1)} reshape(f32[4,1152]{1,0:T(4,128)S(1)} %reduce.11) | data formatting | bytes 36864
  78.9 2.7 %all-to-all-done.1 = f32[4,1,1152]{2,1,0:T(1,128)S(1)} async-done(((f32[4,1,1152]{2,1,0:T(1,128)}), f32[4,1,1152]{2,1,0:T(1,128)S(1)}, u32[]{:S(2)}, u32[]{:S(2)}) %all-to-all-start.1) | async-done | bytes 18464 | tf_op jit(solution)/shard_map/all_to_all | solution.py:87
  82.2 1.8 %reshape.499 = f32[2304,1,2]{2,1,0:T(1,128)S(1)} reshape(f32[4,1152]{1,0:T(4,128)S(1)} %reduce.13) | data formatting | bytes 36864
  84.8 1.0 fusion.4
  85.8 1.3 %broadcast_multiply_fusion = f32[128,16]{0,1:T(8,128)} fusion(f32[128,16]{0,1:T(8,128)} %reduce-scatter.5.cloned.1.call-done), kind=kLoop, calls=%fused_computation.117 | loop fusion | flops 2048 | bytes 16384 | tf_op jit(solution)/shard_map/mul | solution.py:104
  87.1 29.7 %reduce-scatter.3.cloned.1.call-done = f32[16,128]{1,0:T(8,128)} async-done(((f32[256,128]{1,0:T(8,128)}), f32[16,128]{1,0:T(8,128)}) %reduce-scatter.3.cloned.1.call-update) | async-done | bytes 8208 | tf_op jit(solution)/shard_map/reduce_scatter | solution.py:92
  116.8 1.3 %broadcast_multiply_fusion.1 = f32[16,128]{1,0:T(8,128)} fusion(f32[16,128]{1,0:T(8,128)} %reduce-scatter.3.cloned.1.call-done), kind=kLoop, calls=%fused_computation.118 | loop fusion | flops 2048 | bytes 16384 | tf_op jit(solution)/shard_map/mul | solution.py:104
  (50 shorter events, 9.4 us)
Async XLA Ops:
  7.2 78.7 %reduce-scatter.5.cloned.1.call-start = ((), (), s32[]{:S(2)}) async-start(), calls=%async_computation.5 | async-start | bytes 73728 | tf_op jit(solution)/shard_map/reduce_scatter | solution.py:91
  15.8 1.8 %copy-start.2 = (f32[48,2560]{1,0:T(8,128)S(1)}, f32[48,2560]{1,0:T(8,128)}, u32[]{:S(2)}) copy-start(f32[48,2560]{1,0:T(8,128)} %fusion.68) | copy-start | bytes 1474564
  19.7 1.5 %copy-start = (f32[2560,128]{0,1:T(8,128)S(1)}, f32[2560,128]{0,1:T(8,128)}, u32[]{:S(2)}) copy-start(f32[2560,128]{0,1:T(8,128)} %convolution_bitcast_fusion.1) | copy-start | bytes 3932164
  21.2 1.5 %copy-start.1 = (f32[2560,128]{1,0:T(8,128)S(1)}, f32[2560,128]{1,0:T(8,128)}, u32[]{:S(2)}) copy-start(f32[2560,128]{1,0:T(8,128)} %copy.24) | copy-start | bytes 3932164
  51.5 19.3 %all-to-all-start = ((f32[4,1,1152]{2,1,0:T(1,128)}), f32[4,1,1152]{2,1,0:T(1,128)S(1)}, u32[]{:S(2)}, u32[]{:S(2)}) async-start(f32[4,1,1152]{2,1,0:T(1,128)} %reshape.496), calls=%async_computation | async-start | bytes 36864 | tf_op jit(solution)/shard_map/all_to_all | solution.py:87
  56.4 60.4 %reduce-scatter.3.cloned.1.call-start = ((), (), s32[]{:S(2)}) async-start(), calls=%async_computation.4 | async-start | bytes 139264 | tf_op jit(solution)/shard_map/reduce_scatter | solution.py:92
  70.8 10.7 %all-to-all-start.1 = ((f32[4,1,1152]{2,1,0:T(1,128)}), f32[4,1,1152]{2,1,0:T(1,128)S(1)}, u32[]{:S(2)}, u32[]{:S(2)}) async-start(f32[4,1,1152]{2,1,0:T(1,128)} %reshape.498), calls=%async_computation.1 | async-start | bytes 36864 | tf_op jit(solution)/shard_map/all_to_all | solution.py:87
Sparse Core Ops, SparseCore 0:
  13.2 32.7 reduce-scatter.4
  61.1 55.6 reduce-scatter.2
where the time goes:
time: 125 us
  waiting for transfers between devices  32.4 us (26%)
  other arithmetic  29.6 us (24%)
  local copies, waits for them, and re-layouts  16.8 us (13%)
  between operations  15.6 us (12%)
  blocking collectives  13.2 us (11%)
  starting transfers between devices  10 us (8%)
  matrix products  7.37 us (6%)
    reduce_scatter x1, waiting for transfers between devices, finish(): lax.psum_scatter(part_y, ('gx', 'gz', 'vert'), scatter_dimension=0, tiled...  29.7 us
    unnamed x2, other arithmetic  20.9 us
    psum x1, blocking collectives, finish(): summed, sum_x = lax.psum((partial_core, part_x), ('gz', 'vert'))  13.2 us
    all_to_all x2, starting transfers between devices, finish(): lax.all_to_all(summed, 'gx', split_axis=0, concat_axis=2, tiled=True)  9.97 us
    unnamed x11, local copies, waits for them, and re-layouts  6.86 us
    dot_general x2, local copies, waits for them, and re-layouts, batch_terms(): jnp.dot(rows_z, az_low, preferred_element_type=jnp.float32)  2.95 us
    psum x2, local copies, waits for them, and re-layouts, finish(): summed, sum_x = lax.psum((partial_core, part_x), ('gz', 'vert'))  2.89 us
    all_to_all x2, waiting for transfers between devices, finish(): lax.all_to_all(summed, 'gx', split_axis=0, concat_axis=2, tiled=True)  2.68 us
  transfers between devices with their start and end apart: 4, of which 2 were waited for; matrix products, arithmetic and copies ran while one was open for 38% of the time, Pallas kernels for 0%

commit v1 on v0

--- a/solution.py
+++ b/solution.py
@@ -84,7 +84,15 @@
         ).astype(jnp.float32)
         core = jnp.einsum(
             "rex,ax->rea",
-            lax.all_to_all(summed, "gx", split_axis=0, concat_axis=2, tiled=True),
+            jnp.concatenate(
+                jax.lax.all_to_all(
+                    jnp.stack(jnp.split(summed, jax.lax.axis_size("gx"), 0), 0),
+                    axis_name="gx",
+                    concat_axis=0,
+                    split_axis=0,
+                ),
+                2,
+            ),
             phx_whole,
             precision=highest,
         )

time: 125 us -> 112 us (0.90)
  other arithmetic: 29.6 us -> 8.57 us
  waiting for transfers between devices: 32.4 us -> 52.6 us
  local copies, waits for them, and re-layouts: 16.8 us -> 6.42 us
  starting transfers between devices: 10 us -> 8.22 us
    unnamed x2 -> x0, other arithmetic: 20.9 us -> none
    reduce_scatter x1, waiting for transfers between devices: 29.7 us -> 43.6 us  [finish(): lax.psum_scatter(part_y, ('gx', 'gz', 'vert'), scatter_dimension=0, tiled...]
    unnamed x11 -> x6, local copies, waits for them, and re-layouts: 6.86 us -> 0.01 us
    all_to_all x2, waiting for transfers between devices: 2.68 us -> 8.94 us  [finish(): jax.lax.all_to_all(jnp.stack(jnp.split(summed, jax.lax.axis_size('gx'), 0...]
    psum x2 -> x0, local copies, waits for them, and re-layouts: 2.89 us -> none  [finish(): summed, sum_x = lax.psum((partial_core, part_x), ('gz', 'vert'))]
    all_to_all x2, starting transfers between devices: 9.97 us -> 8.19 us  [finish(): jax.lax.all_to_all(jnp.stack(jnp.split(summed, jax.lax.axis_size('gx'), 0...]
    all_to_all x2 -> x0, other arithmetic: 1.4 us -> none  [finish(): lax.all_to_all(summed, 'gx', split_axis=0, concat_axis=2, tiled=True)]
  transfers between devices with their start and end apart: 4 -> 4, of which waited for: 2 -> 3; matrix products, arithmetic and copies ran while one was open for 38% -> 14% of each run, Pallas kernels for 0% -> 0%
where the time goes in v1:
time: 112 us
  waiting for transfers between devices  52.6 us (47%)
  between operations  15.5 us (14%)
  blocking collectives  13.2 us (12%)
  other arithmetic  8.57 us (8%)
  starting transfers between devices  8.22 us (7%)
  matrix products  7.36 us (7%)
  local copies, waits for them, and re-layouts  6.42 us (6%)
    reduce_scatter x1, waiting for transfers between devices, finish(): lax.psum_scatter(part_y, ('gx', 'gz', 'vert'), scatter_dimension=0, tiled...  43.6 us
    psum x1, blocking collectives, finish(): summed, sum_x = lax.psum((partial_core, part_x), ('gz', 'vert'))  13.2 us
    all_to_all x2, waiting for transfers between devices, finish(): jax.lax.all_to_all(jnp.stack(jnp.split(summed, jax.lax.axis_size('gx'), 0...  8.94 us
    all_to_all x2, starting transfers between devices, finish(): jax.lax.all_to_all(jnp.stack(jnp.split(summed, jax.lax.axis_size('gx'), 0...  8.19 us
    dot_general x2, local copies, waits for them, and re-layouts, batch_terms(): jnp.dot(rows_z, az_low, preferred_element_type=jnp.float32)  2.95 us
  transfers between devices with their start and end apart: 4, of which 3 were waited for; matrix products, arithmetic and copies ran while one was open for 14% of the time, Pallas kernels for 0%

profile of v1, /device:TPU:0, one launch (start us, length us, event | category | flops | bytes accessed | tf_op | source)
XLA Modules:
  0.0 111.8 jit_solution(16672092749914957688)
XLA Ops:
  7.2 1.3 %fusion.297 = (s32[1]{0:T(128)}, s32[1]{0:T(128)}) fusion(s32[2]{0:T(128)} %param.4), kind=kLoop, calls=%fused_computation.355 | loop fusion | bytes 16 | tf_op jit(solution)/shard_map/slice | solution.py:38
  8.5 0.8 multiply_bitcast_fusion
  9.6 1.4 %fusion.296 = (bf16[1,2,5,1,256,128]{5,4,3,2,1,0:T(8,128)(2,1)S(1)}, bf16[1,2,5,1,256,128]{5,4,3,2,1,0:T(8,128)(2,1)S(1)}) fusion(bf16[2,2,5,1,256,128]{5,4,3,2,1,0:T(8,128)(2,1)} %param.3), kind=kLoop, calls=%fused_computation.354 | loop fusion | bytes 2621440 | tf_op jit(solution)/shard_map/slice | solution.py:52
  12.4 0.6 add.598
  13.8 1.2 %fusion.70 = f32[48,2560]{1,0:T(8,128)} fusion(bf16[2560,128]{1,0:T(8,128)(2,1)S(1)} %bitcast.120, s32[]{:T(128)} %bitcast.15, s32[128]{0:T(128)S(1)} %iota_add_fusion.2, s32[48]{0:T(128)S(1)} %iota_multiply_fusion.2), kind=kOutput, calls=%fused_computation.90 | convolution fusion | flops 31574016 | bytes 1147588 | tf_op jit(solution)/shard_map/dot_general | solution.py:71
  15.8 1.5 %convolution_bitcast_fusion.1 = f32[2560,128]{0,1:T(8,128)} fusion(bf16[2560,128]{1,0:T(8,128)(2,1)S(1)} %bitcast.121, s32[]{:T(128)} %bitcast, s32[128]{0:T(128)S(1)} %broadcast_multiply_fusion.3), kind=kOutput, calls=%fused_computation.1 | convolution fusion | flops 84197376 | bytes 1966596 | tf_op jit(solution)/shard_map/dot_general | solution.py:61
  17.6 0.6 convolution_bitcast_fusion.5
  18.7 0.6 convolution_bitcast_fusion.4
  19.8 1.5 %copy.38 = f32[2560,128]{1,0:T(8,128)} copy(f32[2560,128]{0,1:T(8,128)S(1)} %convolution_bitcast_fusion) | data formatting | bytes 2621440 | tf_op jit(solution)/shard_map/dot_general | solution.py:61
  21.2 1.5 %copy.36 = f32[2560,128]{1,0:T(8,128)} copy(f32[2560,128]{0,1:T(8,128)S(1)} %copy-done) | data formatting | bytes 2621440 | tf_op jit(solution)/shard_map/dot_general | solution.py:61
  22.7 1.7 %multiply_reduce_fusion = (f32[256,128]{1,0:T(8,128)S(1)}, f32[10,128]{1,0:T(8,128)S(1)}, f32[10,128]{1,0:T(8,128)S(1)}, f32[256,128]{1,0:T(8,128)S(1)}) fusion(f32[10,1,256,128]{3,2,0,1:T(8,128)S(1)} %bitcast.125, f32[10,128]{1,0:T(8,128)S(1)} %get-tuple-element.31, f32[256,128]{1,0:T(8,128)S(1)} %copy.37, f32[10,1,256,128]{3,2,0,1:T(8,128)} %bitcast.126, ...), kind=kLoop, calls=%fused_computation.2 | loop fusion | flops 2553344 | bytes 3035136 | tf_op jit(solution)/shard_map/reduce_sum | solution.py:69
  24.6 13.2 %all-reduce = (f32[1,128]{1,0:T(1,128)S(1)}, f32[2304,2,1]{0,1,2:T(2,128)S(1)}, f32[2304,2,1]{0,1,2:T(2,128)S(1)}) all-reduce(f32[1,128]{1,0:T(1,128)S(1)} %add_bitcast_fusion, f32[2304,2,1]{0,1,2:T(2,128)S(1)} %reshape.498, f32[2304,2,1]{0,1,2:T(2,128)S(1)} %reshape.503), channel_id=1, replica_groups=mesh['groups'=2,'gx'=4,'gz'=2,'vert'=2] {'gz','vert'}, use_global_device_ids=true, to_apply=%region_2.0 | all-reduce | flops 9344 | bytes 74752 | tf_op jit(solution)/shard_map/psum | solution.py:81
  37.8 0.6 pad_maximum_fusion
  38.4 4.9 %all-to-all-start = ((f32[4,576,2,1]{1,2,3,0:T(2,128)}), f32[4,576,2,1]{1,2,3,0:T(2,128)S(1)}, u32[]{:S(2)}, u32[]{:S(2)}) async-start(f32[4,576,2,1]{1,2,3,0:T(2,128)} %pad_maximum_fusion), calls=%async_computation | async-start | bytes 40960 | tf_op jit(solution)/shard_map/all_to_all | solution.py:88
  43.4 0.7 add.597
  44.1 0.5 broadcast_multiply_fusion.2
  44.7 0.6 pad_maximum_fusion.1
  45.3 3.7 %all-to-all-done = f32[4,576,2,1]{1,2,3,0:T(2,128)S(1)} async-done(((f32[4,576,2,1]{1,2,3,0:T(2,128)}), f32[4,576,2,1]{1,2,3,0:T(2,128)S(1)}, u32[]{:S(2)}, u32[]{:S(2)}) %all-to-all-start) | async-done | bytes 18464 | tf_op jit(solution)/shard_map/all_to_all | solution.py:88
  49.0 3.3 %all-to-all-start.1 = ((f32[4,576,2,1]{1,2,3,0:T(2,128)}), f32[4,576,2,1]{1,2,3,0:T(2,128)S(1)}, u32[]{:S(2)}, u32[]{:S(2)}) async-start(f32[4,576,2,1]{1,2,3,0:T(2,128)} %pad_maximum_fusion.1), calls=%async_computation.1 | async-start | bytes 40960 | tf_op jit(solution)/shard_map/all_to_all | solution.py:88
  52.6 5.3 %all-to-all-done.1 = f32[4,576,2,1]{1,2,3,0:T(2,128)S(1)} async-done(((f32[4,576,2,1]{1,2,3,0:T(2,128)}), f32[4,576,2,1]{1,2,3,0:T(2,128)S(1)}, u32[]{:S(2)}, u32[]{:S(2)}) %all-to-all-start.1) | async-done | bytes 18464 | tf_op jit(solution)/shard_map/all_to_all | solution.py:88
  57.8 1.0 fusion.4
  58.8 1.3 %broadcast_multiply_fusion = f32[128,16]{0,1:T(8,128)} fusion(f32[128,16]{0,1:T(8,128)} %reduce-scatter.5.cloned.1.call-done), kind=kLoop, calls=%fused_computation.129 | loop fusion | flops 2048 | bytes 16384 | tf_op jit(solution)/shard_map/mul | solution.py:112
  60.1 43.6 %reduce-scatter.3.cloned.1.call-done = f32[16,128]{1,0:T(8,128)} async-done(((f32[256,128]{1,0:T(8,128)}), f32[16,128]{1,0:T(8,128)}) %reduce-scatter.3.cloned.1.call-update) | async-done | bytes 8208 | tf_op jit(solution)/shard_map/reduce_scatter | solution.py:100
  103.7 1.3 %broadcast_multiply_fusion.1 = f32[16,128]{1,0:T(8,128)} fusion(f32[16,128]{1,0:T(8,128)} %reduce-scatter.3.cloned.1.call-done), kind=kLoop, calls=%fused_computation.130 | loop fusion | flops 2048 | bytes 16384 | tf_op jit(solution)/shard_map/mul | solution.py:112
  (41 shorter events, 3.8 us)
Async XLA Ops:
  7.2 51.7 %reduce-scatter.5.cloned.1.call-start = ((), (), s32[]{:S(2)}) async-start(), calls=%async_computation.5 | async-start | bytes 73728 | tf_op jit(solution)/shard_map/reduce_scatter | solution.py:99
  15.8 1.8 %copy-start.2 = (f32[48,2560]{1,0:T(8,128)S(1)}, f32[48,2560]{1,0:T(8,128)}, u32[]{:S(2)}) copy-start(f32[48,2560]{1,0:T(8,128)} %fusion.70) | copy-start | bytes 1474564
  19.7 1.5 %copy-start = (f32[2560,128]{0,1:T(8,128)S(1)}, f32[2560,128]{0,1:T(8,128)}, u32[]{:S(2)}) copy-start(f32[2560,128]{0,1:T(8,128)} %convolution_bitcast_fusion.1) | copy-start | bytes 3932164
  21.2 1.5 %copy-start.1 = (f32[2560,128]{1,0:T(8,128)S(1)}, f32[2560,128]{1,0:T(8,128)}, u32[]{:S(2)}) copy-start(f32[2560,128]{1,0:T(8,128)} %copy.38) | copy-start | bytes 3932164
  38.4 10.6 %all-to-all-start = ((f32[4,576,2,1]{1,2,3,0:T(2,128)}), f32[4,576,2,1]{1,2,3,0:T(2,128)S(1)}, u32[]{:S(2)}, u32[]{:S(2)}) async-start(f32[4,576,2,1]{1,2,3,0:T(2,128)} %pad_maximum_fusion), calls=%async_computation | async-start | bytes 40960 | tf_op jit(solution)/shard_map/all_to_all | solution.py:88
  43.4 60.4 %reduce-scatter.3.cloned.1.call-start = ((), (), s32[]{:S(2)}) async-start(), calls=%async_computation.4 | async-start | bytes 139264 | tf_op jit(solution)/shard_map/reduce_scatter | solution.py:100
  49.0 8.9 %all-to-all-start.1 = ((f32[4,576,2,1]{1,2,3,0:T(2,128)}), f32[4,576,2,1]{1,2,3,0:T(2,128)S(1)}, u32[]{:S(2)}, u32[]{:S(2)}) async-start(f32[4,576,2,1]{1,2,3,0:T(2,128)} %pad_maximum_fusion.1), calls=%async_computation.1 | async-start | bytes 40960 | tf_op jit(solution)/shard_map/all_to_all | solution.py:88
Sparse Core Ops, SparseCore 0:
  13.2 32.7 reduce-scatter.4
  49.8 53.8 reduce-scatter.2
